TPU v7x, 512 devices: a whole 4x4x16 slice. The times are simulated.
512 devices in a mesh: pix: 64 (over z, x), tm: 8 (over y, core).
Axes of the slice: x: 4, y: 4, z: 16, core: 2. Of those that a mesh axis runs over, the one named last changes fastest.
Arguments:
- movie: bfloat16 [131072, 2048], P('pix', 'tm'), may hold values from -6 to 6
- traces: bfloat16 [2048, 2048], P('pix', 'tm'), may hold values from 0 to 2
- footprints: bfloat16 [16384, 128], P('pix'), may hold values from 0 to 0.2
- slot_block: int32 [16384], P('pix'), may hold values from 0 to 15
- slot_neuron: int32 [16384], P('pix'), may hold values from 0 to 31
- bucket_fill: int32 [64, 64], P('pix'), may hold values from 1 to 4, as said below
Outputs:
- traces_new: bfloat16 [2048, 2048], P('pix', 'tm')
- footprints_new: float32 [16384, 128], P('pix')
Inputs may be any that keep to these rules, and one draw needn't show every extreme that they name: `bucket_fill`: A tile has at most 4 used slots for one owner; in every draw some owner gets 4 from every tile, and every tile fills 4 for some owner.
All inputs are finite; a program needn't handle non-finite values.
Results may differ from a plain program's by a relative error of at most 0.0049.
Values may be sent and summed in bfloat16 or wider, within the bound.
No kernel may reach another device: no remote copies, remote signals or barrier semaphores. Data moves between devices by JAX's collectives and lax.ppermute only.
A program may use at most 64 MiB of HBM per device.

v0:
```python
import jax
import jax.numpy as jnp
from jax import lax
from jax.sharding import PartitionSpec as P

BLOCK = 128


def local(movie, traces, footprints, slot_block, slot_neuron, bucket_fill):
    pix_count = lax.axis_size("pix")
    slot_total = footprints.shape[0]
    capacity = slot_total // pix_count
    neur_local = traces.shape[0]
    block_count = movie.shape[0] // BLOCK
    slot_index = jnp.arange(slot_total, dtype=jnp.int32)
    bucket_of = slot_index // capacity
    position = slot_index % capacity
    owner_match = bucket_of[:, None] == jnp.arange(pix_count, dtype=jnp.int32)[None, :]
    fill_slot = jnp.sum(jnp.where(owner_match, bucket_fill[0][None, :], 0), axis=1)
    usable = position < fill_slot
    masked = footprints * usable[:, None].astype(jnp.bfloat16)
    block_pick = slot_block[:, None] == jnp.arange(block_count, dtype=jnp.int32)[None, :]
    dense_map = (block_pick.astype(jnp.bfloat16)[:, :, None] * masked[:, None, :]).reshape(
        slot_total, block_count * BLOCK
    )
    asked_ids = lax.all_to_all(
        slot_neuron.reshape(pix_count, capacity), "pix", split_axis=0, concat_axis=0, tiled=True
    )
    asked_flat = asked_ids.reshape(slot_total)

    def slot_rows(source_rows):
        gathered = lax.all_gather(source_rows, "pix", axis=0, tiled=True)
        global_row = bucket_of * neur_local + slot_neuron
        return gathered[global_row]

    def residual_of(slot_traces):
        rebuilt = lax.dot_general(
            dense_map, slot_traces, (((0,), (0,)), ((), ())), preferred_element_type=jnp.float32
        )
        return (movie.astype(jnp.float32) - rebuilt).astype(jnp.bfloat16)

    slot_traces = slot_rows(traces)
    residual = residual_of(slot_traces)
    projection = jnp.dot(dense_map, residual, preferred_element_type=jnp.float32)
    slot_power = jnp.sum(masked.astype(jnp.float32) ** 2, axis=1)
    got_proj, got_power = (
        lax.all_to_all(
            projection.reshape(pix_count, capacity, projection.shape[1]),
            "pix",
            split_axis=0,
            concat_axis=0,
            tiled=True,
        ),
        lax.all_to_all(
            slot_power.reshape(pix_count, capacity), "pix", split_axis=0, concat_axis=0, tiled=True
        ),
    )
    owner_pick = (jnp.arange(neur_local, dtype=jnp.int32)[:, None] == asked_flat[None, :]).astype(
        jnp.float32
    )
    summed = jnp.dot(
        owner_pick,
        got_proj.reshape(slot_total, projection.shape[1]),
        precision=lax.Precision.HIGHEST,
    )
    power = jnp.dot(owner_pick, got_power.reshape(slot_total), precision=lax.Precision.HIGHEST)
    updated = jnp.maximum(
        0.0, traces.astype(jnp.float32) + summed / jnp.maximum(power, 0.5)[:, None]
    ).astype(jnp.bfloat16)
    slot_updated = slot_rows(updated)
    residual_two = residual_of(slot_updated)
    products = lax.dot_general(
        residual_two, slot_updated, (((1,), (1,)), ((), ())), preferred_element_type=jnp.float32
    )
    numerator = jnp.einsum(
        "bps,sb->sp",
        products.reshape(block_count, BLOCK, slot_total),
        block_pick.astype(jnp.float32),
        precision=lax.Precision.HIGHEST,
    )
    trace_power = jnp.sum(slot_updated.astype(jnp.float32) ** 2, axis=1)
    numer_all, power_all = lax.psum((numerator, trace_power), "tm")
    grown = jnp.maximum(0.0, masked.astype(jnp.float32) + numer_all / (power_all + 1e-06)[:, None])
    return (updated, jnp.where(usable[:, None], grown, 0.0))


def solution(mesh):
    return jax.shard_map(
        local,
        mesh=mesh,
        in_specs=(
            P("pix", "tm"),
            P("pix", "tm"),
            P("pix", None),
            P("pix"),
            P("pix"),
            P("pix", None),
        ),
        out_specs=(P("pix", "tm"), P("pix", None)),
        check_vma=False,
    )
```

profile of v0, /device:TPU:2, one launch (start us, length us, event | category | flops | bytes accessed | tf_op | source)
XLA Modules:
  0.0 437.4 jit_solution(8261402427538340543)
XLA Ops:
  7.2 0.0 all-gather.3.cloned.1.call-start
  7.2 0.7 all-gather.3.cloned.1.call-update
  7.9 1.4 all_to_all.15
  9.3 18.6 %all-to-all-start = ((s32[64,1,4]{2,1,0:T(1,128)}), s32[64,1,4]{2,1,0:T(1,128)S(1)}, u32[]{:S(2)}, u32[]{:S(2)}) async-start(s32[64,1,4]{2,1,0:T(1,128)} %bitcast), calls=%async_computation | async-start | bytes 65536 | tf_op jit(solution)/shard_map/all_to_all | solution.py:26
  27.9 0.7 select_reduce_fusion
  28.7 0.7 compare_select_fusion
  29.4 0.8 fusion.24
  30.2 1.0 fusion.21
  31.2 0.0 copy-start
  31.2 0.7 broadcast_multiply_fusion
  31.9 0.7 all_to_all.18
  32.7 0.3 mul.38
  32.9 121.4 %all-gather.3.cloned.1.call-done = bf16[2048,256]{1,0:T(8,128)(2,1)} async-done(((bf16[32,256]{1,0:T(8,128)(2,1)}), bf16[2048,256]{1,0:T(8,128)(2,1)}) %all-gather.3.cloned.1.call-update) | async-done | bytes 1048592 | tf_op jit(solution)/shard_map/all_gather | solution.py:32
  154.3 2.3 gather_fusion
  156.7 0.0 all-to-all-done
  156.7 11.4 %all-to-all-start.2 = ((f32[64,1,4]{2,1,0:T(1,128)}), f32[64,1,4]{2,1,0:T(1,128)S(1)}, u32[]{:S(2)}, u32[]{:S(2)}) async-start(f32[64,1,4]{2,1,0:T(1,128)} %bitcast.3), calls=%async_computation.2 | async-start | bytes 65536 | tf_op jit(solution)/shard_map/all_to_all | solution.py:54
  168.1 0.0 copy-done
  168.1 0.0 copy-start.1
  168.1 2.0 fusion.11
  170.1 1.8 copy.16
  171.9 10.0 %all-to-all-done.2 = f32[64,1,4]{2,1,0:T(1,128)S(1)} async-done(((f32[64,1,4]{2,1,0:T(1,128)}), f32[64,1,4]{2,1,0:T(1,128)S(1)}, u32[]{:S(2)}, u32[]{:S(2)}) %all-to-all-start.2) | async-done | bytes 1056 | tf_op jit(solution)/shard_map/all_to_all | solution.py:54
  182.0 5.2 %all-to-all-start.1 = ((f32[64,4,256]{2,1,0:T(4,128)}), f32[64,4,256]{2,1,0:T(4,128)S(1)}, u32[]{:S(2)}, u32[]{:S(2)}) async-start(f32[64,4,256]{2,1,0:T(4,128)} %copy.16), calls=%async_computation.1 | async-start | bytes 524288 | tf_op jit(solution)/shard_map/all_to_all | solution.py:47
  187.2 0.0 all-gather.5.cloned.1.call-start
  187.3 0.5 broadcast.107
  187.8 0.7 reduce.7
  188.5 0.1 eq.48
  188.6 0.5 broadcast.106
  189.1 0.7 reduce.6
  189.9 0.1 reshape.111
  190.0 0.1 fusion.7
  190.1 15.0 %all-to-all-done.1 = f32[64,4,256]{2,1,0:T(4,128)S(1)} async-done(((f32[64,4,256]{2,1,0:T(4,128)}), f32[64,4,256]{2,1,0:T(4,128)S(1)}, u32[]{:S(2)}, u32[]{:S(2)}) %all-to-all-start.1) | async-done | bytes 262176 | tf_op jit(solution)/shard_map/all_to_all | solution.py:47
  205.1 0.1 reshape.89
  205.2 0.0 copy-done.1
  205.2 0.8 fusion.6
  206.0 0.0 all-gather.5.cloned.1.call-update
  206.1 0.0 all-reduce.2.cloned.1.call-start
  206.1 130.1 %all-gather.5.cloned.1.call-done = bf16[2048,256]{1,0:T(8,128)(2,1)} async-done(((bf16[32,256]{1,0:T(8,128)(2,1)}), bf16[2048,256]{1,0:T(8,128)(2,1)}) %all-gather.5.cloned.1.call-update) | async-done | bytes 1048592 | tf_op jit(solution)/shard_map/all_gather | solution.py:32
  336.2 2.3 gather_fusion.1
  338.6 0.1 multiply_reduce_fusion
  338.7 2.1 fusion.3
  340.8 12.4 %psum.15 = f32[256]{0:T(256)S(1)} all-reduce(f32[256]{0:T(256)S(1)} %multiply_reduce_fusion), channel_id=1, replica_groups=mesh['pix'=64,'tm'=8] {'tm'}, use_global_device_ids=true, to_apply=%region_4.5 | all-reduce | flops 256 | bytes 2048 | tf_op jit(solution)/shard_map/psum | solution.py:82
  353.2 2.0 copy.18
  355.2 3.5 fusion.19
  358.7 0.0 all-reduce.2.cloned.1.call-update
  358.7 70.4 %all-reduce.2.cloned.1.call-done = f32[256,128]{1,0:T(8,128)} async-done(((f32[256,128]{1,0:T(8,128)}), f32[256,128]{1,0:T(8,128)}) %all-reduce.2.cloned.1.call-update) | async-done | bytes 131088 | tf_op jit(solution)/shard_map/psum | solution.py:82
  429.2 1.7 fusion.23
  (4 shorter events, 0.0 us)
Async XLA Ops:
  7.2 147.2 %all-gather.3.cloned.1.call-start = ((), (), s32[]{:S(2)}) async-start(), calls=%async_computation.3 | async-start | bytes 1064960 | tf_op jit(solution)/shard_map/all_gather | solution.py:32
  9.3 147.4 %all-to-all-start = ((s32[64,1,4]{2,1,0:T(1,128)}), s32[64,1,4]{2,1,0:T(1,128)S(1)}, u32[]{:S(2)}, u32[]{:S(2)}) async-start(s32[64,1,4]{2,1,0:T(1,128)} %bitcast), calls=%async_computation | async-start | bytes 65536 | tf_op jit(solution)/shard_map/all_to_all | solution.py:26
  31.2 136.9 %copy-start = (bf16[2048,256]{1,0:T(8,128)(2,1)S(1)}, bf16[2048,256]{1,0:T(8,128)(2,1)}, u32[]{:S(2)}) copy-start(bf16[2048,256]{1,0:T(8,128)(2,1)} %param.6) | copy-start | bytes 3145732
  156.7 25.3 %all-to-all-start.2 = ((f32[64,1,4]{2,1,0:T(1,128)}), f32[64,1,4]{2,1,0:T(1,128)S(1)}, u32[]{:S(2)}, u32[]{:S(2)}) async-start(f32[64,1,4]{2,1,0:T(1,128)} %bitcast.3), calls=%async_computation.2 | async-start | bytes 65536 | tf_op jit(solution)/shard_map/all_to_all | solution.py:54
  168.1 37.1 %copy-start.1 = (bf16[32,256]{1,0:T(8,128)(2,1)S(1)}, bf16[32,256]{1,0:T(8,128)(2,1)}, u32[]{:S(2)}) copy-start(bf16[32,256]{1,0:T(8,128)(2,1)} %param.7) | copy-start | bytes 49156
  182.0 23.1 %all-to-all-start.1 = ((f32[64,4,256]{2,1,0:T(4,128)}), f32[64,4,256]{2,1,0:T(4,128)S(1)}, u32[]{:S(2)}, u32[]{:S(2)}) async-start(f32[64,4,256]{2,1,0:T(4,128)} %copy.16), calls=%async_computation.1 | async-start | bytes 524288 | tf_op jit(solution)/shard_map/all_to_all | solution.py:47
  187.2 149.0 %all-gather.5.cloned.1.call-start = ((), (), s32[]{:S(2)}) async-start(), calls=%async_computation.4 | async-start | bytes 1064960 | tf_op jit(solution)/shard_map/all_gather | solution.py:32
  206.1 223.1 %all-reduce.2.cloned.1.call-start = ((), (), s32[]{:S(2)}) async-start(), calls=%async_computation.5 | async-start | bytes 262144 | tf_op jit(solution)/shard_map/psum | solution.py:82
Sparse Core Ops, SparseCore 0:
  10.9 143.3 all-gather.2
  206.2 130.0 all-gather.4
  358.8 70.2 all-reduce.1
where the time goes:
time: 438 us; the launch traced here: 437 us
  waiting for transfers between devices  348 us (79%)
  starting transfers between devices  35.4 us (8%)
  between operations  13.9 us (3%)
  blocking collectives  12.4 us (3%)
  local copies, waits for them, and re-layouts  12.2 us (3%)
  matrix products  8.5 us (2%)
  other arithmetic  7.22 us (2%)
    all_gather x2, waiting for transfers between devices, slot_rows(): gathered = lax.all_gather(source_rows, 'pix', axis=0, tiled=True)  252 us
    psum x1, waiting for transfers between devices, local(): numer_all, power_all = lax.psum((numerator, trace_power), 'tm')  70.4 us
    all_to_all x1, starting transfers between devices, local(): lax.all_to_all(slot_neuron.reshape(pix_count, capacity), 'pix', split_axi...  18.6 us
    all_to_all x1, waiting for transfers between devices, local(): lax.all_to_all(projection.reshape(pix_count, capacity, projection.shape[1...  15 us
    psum x1, blocking collectives, local(): numer_all, power_all = lax.psum((numerator, trace_power), 'tm')  12.4 us
    all_to_all x1, starting transfers between devices, local(): lax.all_to_all(slot_power.reshape(pix_count, capacity), 'pix', split_axis...  11.4 us
    all_to_all x1, waiting for transfers between devices, local(): lax.all_to_all(slot_power.reshape(pix_count, capacity), 'pix', split_axis...  10 us
  transfers between devices with their start and end apart: 6, of which 5 were waited for; matrix products, arithmetic and copies ran while one was open for 3% of the time, Pallas kernels for 0%

commit v1 on v0

--- a/solution.py
+++ b/solution.py
@@ -4,6 +4,11 @@
 from jax.sharding import PartitionSpec as P
 
 BLOCK = 128
+
+
+def all_by_exchange(x, axis, dim):
+    stack = jnp.stack([x] * lax.axis_size(axis))
+    return jnp.concatenate(lax.all_to_all(stack, axis, 0, 0), axis=dim)
 
 
 def local(movie, traces, footprints, slot_block, slot_neuron, bucket_fill):
@@ -29,7 +34,7 @@
     asked_flat = asked_ids.reshape(slot_total)
 
     def slot_rows(source_rows):
-        gathered = lax.all_gather(source_rows, "pix", axis=0, tiled=True)
+        gathered = all_by_exchange(source_rows, "pix", 0)
         global_row = bucket_of * neur_local + slot_neuron
         return gathered[global_row]
 

time: 438 us -> 300 us (0.68)
  waiting for transfers between devices: 348 us -> 155 us
  blocking collectives: 12.4 us -> 70.1 us
    all_gather x2 -> x0, waiting for transfers between devices: 252 us -> none  [slot_rows(): gathered = lax.all_gather(source_rows, 'pix', axis=0, tiled=True)]
    all_to_all x0 -> x1, blocking collectives: none -> 57.7 us  [all_by_exchange(): return jnp.concatenate(lax.all_to_all(stack, axis, 0, 0), axis=dim)]
    all_to_all x0 -> x1, waiting for transfers between devices: none -> 53.3 us  [all_by_exchange(): return jnp.concatenate(lax.all_to_all(stack, axis, 0, 0), axis=dim)]
    all_to_all x0 -> x1, starting transfers between devices: none -> 18.6 us  [all_by_exchange(): return jnp.concatenate(lax.all_to_all(stack, axis, 0, 0), axis=dim)]
    all_to_all x1, starting transfers between devices: 18.6 us -> 5.95 us  [local(): lax.all_to_all(slot_neuron.reshape(pix_count, capacity), 'pix', split_axi...]
    all_to_all x1, waiting for transfers between devices: 0.01 us -> 10.8 us  [local(): lax.all_to_all(slot_neuron.reshape(pix_count, capacity), 'pix', split_axi...]
    all_to_all x1, starting transfers between devices: 11.4 us -> 5.46 us  [local(): lax.all_to_all(slot_power.reshape(pix_count, capacity), 'pix', split_axis...]
    psum x1, waiting for transfers between devices: 70.4 us -> 65.1 us  [local(): numer_all, power_all = lax.psum((numerator, trace_power), 'tm')]
  transfers between devices with their start and end apart: 6 -> 5, of which waited for: 5 -> 5; matrix products, arithmetic and copies ran while one was open for 3% -> 3% of each run, Pallas kernels for 0% -> 0%
where the time goes in v1:
time: 300 us; the launch traced here: 299 us
  waiting for transfers between devices  155 us (52%)
  blocking collectives  70.1 us (23%)
  starting transfers between devices  35.7 us (12%)
  between operations  14.3 us (5%)
  local copies, waits for them, and re-layouts  11.1 us (4%)
  matrix products  8.42 us (3%)
  other arithmetic  4.37 us (1%)
    psum x1, waiting for transfers between devices, local(): numer_all, power_all = lax.psum((numerator, trace_power), 'tm')  65.1 us
    all_to_all x1, blocking collectives, all_by_exchange(): return jnp.concatenate(lax.all_to_all(stack, axis, 0, 0), axis=dim)  57.7 us
    all_to_all x1, waiting for transfers between devices, all_by_exchange(): return jnp.concatenate(lax.all_to_all(stack, axis, 0, 0), axis=dim)  53.3 us
    all_to_all x1, starting transfers between devices, all_by_exchange(): return jnp.concatenate(lax.all_to_all(stack, axis, 0, 0), axis=dim)  18.6 us
    all_to_all x1, waiting for transfers between devices, local(): lax.all_to_all(projection.reshape(pix_count, capacity, projection.shape[1...  15.9 us
    psum x1, blocking collectives, local(): numer_all, power_all = lax.psum((numerator, trace_power), 'tm')  12.4 us
    all_to_all x1, waiting for transfers between devices, local(): lax.all_to_all(slot_neuron.reshape(pix_count, capacity), 'pix', split_axi...  10.8 us
    all_to_all x1, waiting for transfers between devices, local(): lax.all_to_all(slot_power.reshape(pix_count, capacity), 'pix', split_axis...  10.3 us
  transfers between devices with their start and end apart: 5, of which 5 were waited for; matrix products, arithmetic and copies ran while one was open for 3% of the time, Pallas kernels for 0%

profile of v1, /device:TPU:2, one launch (start us, length us, event | category | flops | bytes accessed | tf_op | source)
XLA Modules:
  0.0 299.3 jit_solution(1654106559460615131)
XLA Ops:
  7.2 0.0 copy-start.4
  7.2 0.0 copy-start.6
  7.2 0.0 copy-start.5
  7.2 0.0 copy-start.3
  7.2 1.9 stack.4
  9.1 18.6 %all-to-all-start.1 = ((bf16[64,32,256]{2,1,0:T(8,128)(2,1)}), bf16[64,32,256]{2,1,0:T(8,128)(2,1)S(1)}, u32[]{:S(2)}, u32[]{:S(2)}) async-start(bf16[64,32,256]{2,1,0:T(8,128)(2,1)} %stack.4), calls=%async_computation.1 | async-start | bytes 2097152 | tf_op jit(solution)/shard_map/all_to_all | solution.py:11
  27.7 0.7 all_to_all.21
  28.5 0.0 copy-done.6
  28.5 0.1 select_reduce_fusion
  28.6 0.1 fusion.24
  28.7 0.2 fusion.21
  28.9 0.0 copy-start
  28.9 0.7 broadcast_multiply_fusion
  29.6 53.3 %all-to-all-done.1 = bf16[64,32,256]{2,1,0:T(8,128)(2,1)S(1)} async-done(((bf16[64,32,256]{2,1,0:T(8,128)(2,1)}), bf16[64,32,256]{2,1,0:T(8,128)(2,1)S(1)}, u32[]{:S(2)}, u32[]{:S(2)}) %all-to-all-start.1) | async-done | bytes 1048608 | tf_op jit(solution)/shard_map/all_to_all | solution.py:11
  82.9 6.0 %all-to-all-start = ((s32[64,1,4]{2,1,0:T(1,128)}), s32[64,1,4]{2,1,0:T(1,128)S(1)}, u32[]{:S(2)}, u32[]{:S(2)}) async-start(s32[64,1,4]{2,1,0:T(1,128)} %bitcast), calls=%async_computation | async-start | bytes 65536 | tf_op jit(solution)/shard_map/all_to_all | solution.py:31
  88.9 0.7 all_to_all.25
  89.6 1.1 mul.38
  90.7 1.1 gather_fusion
  91.8 10.8 %all-to-all-done = s32[64,1,4]{2,1,0:T(1,128)S(1)} async-done(((s32[64,1,4]{2,1,0:T(1,128)}), s32[64,1,4]{2,1,0:T(1,128)S(1)}, u32[]{:S(2)}, u32[]{:S(2)}) %all-to-all-start) | async-done | bytes 1056 | tf_op jit(solution)/shard_map/all_to_all | solution.py:31
  102.7 5.5 %all-to-all-start.3 = ((f32[64,1,4]{2,1,0:T(1,128)}), f32[64,1,4]{2,1,0:T(1,128)S(1)}, u32[]{:S(2)}, u32[]{:S(2)}) async-start(f32[64,1,4]{2,1,0:T(1,128)} %bitcast.4), calls=%async_computation.3 | async-start | bytes 65536 | tf_op jit(solution)/shard_map/all_to_all | solution.py:59
  108.1 0.0 copy-start.1
  108.2 2.5 fusion.11
  110.7 0.9 copy.16
  111.6 10.3 %all-to-all-done.3 = f32[64,1,4]{2,1,0:T(1,128)S(1)} async-done(((f32[64,1,4]{2,1,0:T(1,128)}), f32[64,1,4]{2,1,0:T(1,128)S(1)}, u32[]{:S(2)}, u32[]{:S(2)}) %all-to-all-start.3) | async-done | bytes 1056 | tf_op jit(solution)/shard_map/all_to_all | solution.py:59
  121.9 5.6 %all-to-all-start.2 = ((f32[64,4,256]{2,1,0:T(4,128)}), f32[64,4,256]{2,1,0:T(4,128)S(1)}, u32[]{:S(2)}, u32[]{:S(2)}) async-start(f32[64,4,256]{2,1,0:T(4,128)} %copy.16), calls=%async_computation.2 | async-start | bytes 524288 | tf_op jit(solution)/shard_map/all_to_all | solution.py:52
  127.5 0.0 all-reduce.2.cloned.1.call-start
  127.5 0.5 broadcast.111
  128.0 0.7 reduce.7
  128.8 0.1 eq.48
  128.9 0.5 broadcast.110
  129.4 0.7 reduce.6
  130.1 0.1 reshape.123
  130.2 0.1 fusion.7
  130.3 15.9 %all-to-all-done.2 = f32[64,4,256]{2,1,0:T(4,128)S(1)} async-done(((f32[64,4,256]{2,1,0:T(4,128)}), f32[64,4,256]{2,1,0:T(4,128)S(1)}, u32[]{:S(2)}, u32[]{:S(2)}) %all-to-all-start.2) | async-done | bytes 262176 | tf_op jit(solution)/shard_map/all_to_all | solution.py:52
  146.2 0.1 reshape.100
  146.3 0.2 fusion.6
  146.6 0.0 copy-start.2
  146.6 0.1 stack.5
  146.7 57.7 %all_to_all.33 = bf16[64,32,256]{2,1,0:T(8,128)(2,1)S(1)} all-to-all(bf16[64,32,256]{2,1,0:T(8,128)(2,1)S(1)} %stack.5), channel_id=1, replica_groups=mesh['pix'=64,'tm'=8] {'pix'}, dimensions={0} | all-to-all | bytes 2097152 | tf_op jit(solution)/shard_map/all_to_all | solution.py:11
  204.4 1.2 gather_fusion.1
  205.5 0.1 multiply_reduce_fusion
  205.7 2.1 fusion.3
  207.7 12.4 %psum.15 = f32[256]{0:T(256)S(1)} all-reduce(f32[256]{0:T(256)S(1)} %multiply_reduce_fusion), channel_id=1, replica_groups=mesh['pix'=64,'tm'=8] {'tm'}, use_global_device_ids=true, to_apply=%region_4.5 | all-reduce | flops 256 | bytes 2048 | tf_op jit(solution)/shard_map/psum | solution.py:87
  220.2 2.0 copy.18
  222.2 3.5 %fusion.19 = f32[256,1,128]{2,1,0:T(1,128)} fusion(f32[16,128,256]{1,0,2:T(8,128)} %copy.18, pred[256,16,1]{1,0,2:T(32,128)(4,1)S(1)} %get-tuple-element.6), kind=kOutput, calls=%fused_computation.21 | convolution fusion | flops 6291456 | bytes 2232320 | tf_op jit(solution)/shard_map/bps,sb->sp/dot_general | solution.py:80
  225.6 0.0 all-reduce.2.cloned.1.call-update
  225.7 65.1 %all-reduce.2.cloned.1.call-done = f32[256,128]{1,0:T(8,128)} async-done(((f32[256,128]{1,0:T(8,128)}), f32[256,128]{1,0:T(8,128)}) %all-reduce.2.cloned.1.call-update) | async-done | bytes 131088 | tf_op jit(solution)/shard_map/psum | solution.py:87
  290.8 1.7 fusion.23
  (11 shorter events, 0.0 us)
Async XLA Ops:
  7.2 20.6 %copy-start.4 = (s32[256]{0:T(256)S(1)}, s32[256]{0:T(256)}, u32[]{:S(2)}) copy-start(s32[256]{0:T(256)} %param.10) | copy-start | bytes 3076
  7.2 21.3 %copy-start.6 = (s32[1,64]{1,0:T(1,128)S(1)}, s32[1,64]{1,0:T(1,128)}, u32[]{:S(2)}) copy-start(s32[1,64]{1,0:T(1,128)} %param.11) | copy-start | bytes 772
  7.2 21.4 %copy-start.5 = (s32[256]{0:T(256)S(1)}, s32[256]{0:T(256)}, u32[]{:S(2)}) copy-start(s32[256]{0:T(256)} %param.9) | copy-start | bytes 3076
  7.2 21.5 %copy-start.3 = (bf16[256,128]{1,0:T(8,128)(2,1)S(1)}, bf16[256,128]{1,0:T(8,128)(2,1)}, u32[]{:S(2)}) copy-start(bf16[256,128]{1,0:T(8,128)(2,1)} %param.8) | copy-start | bytes 196612
  9.1 73.8 %all-to-all-start.1 = ((bf16[64,32,256]{2,1,0:T(8,128)(2,1)}), bf16[64,32,256]{2,1,0:T(8,128)(2,1)S(1)}, u32[]{:S(2)}, u32[]{:S(2)}) async-start(bf16[64,32,256]{2,1,0:T(8,128)(2,1)} %stack.4), calls=%async_computation.1 | async-start | bytes 2097152 | tf_op jit(solution)/shard_map/all_to_all | solution.py:11
  28.9 79.3 %copy-start = (bf16[2048,256]{1,0:T(8,128)(2,1)S(1)}, bf16[2048,256]{1,0:T(8,128)(2,1)}, u32[]{:S(2)}) copy-start(bf16[2048,256]{1,0:T(8,128)(2,1)} %param.6) | copy-start | bytes 3145732
  82.9 19.8 %all-to-all-start = ((s32[64,1,4]{2,1,0:T(1,128)}), s32[64,1,4]{2,1,0:T(1,128)S(1)}, u32[]{:S(2)}, u32[]{:S(2)}) async-start(s32[64,1,4]{2,1,0:T(1,128)} %bitcast), calls=%async_computation | async-start | bytes 65536 | tf_op jit(solution)/shard_map/all_to_all | solution.py:31
  102.7 19.2 %all-to-all-start.3 = ((f32[64,1,4]{2,1,0:T(1,128)}), f32[64,1,4]{2,1,0:T(1,128)S(1)}, u32[]{:S(2)}, u32[]{:S(2)}) async-start(f32[64,1,4]{2,1,0:T(1,128)} %bitcast.4), calls=%async_computation.3 | async-start | bytes 65536 | tf_op jit(solution)/shard_map/all_to_all | solution.py:59
  108.1 38.2 %copy-start.1 = (bf16[32,256]{1,0:T(8,128)(2,1)S(1)}, bf16[32,256]{1,0:T(8,128)(2,1)}, u32[]{:S(2)}) copy-start(bf16[32,256]{1,0:T(8,128)(2,1)} %param.7) | copy-start | bytes 49156
  121.9 24.3 %all-to-all-start.2 = ((f32[64,4,256]{2,1,0:T(4,128)}), f32[64,4,256]{2,1,0:T(4,128)S(1)}, u32[]{:S(2)}, u32[]{:S(2)}) async-start(f32[64,4,256]{2,1,0:T(4,128)} %copy.16), calls=%async_computation.2 | async-start | bytes 524288 | tf_op jit(solution)/shard_map/all_to_all | solution.py:52
  127.5 163.3 %all-reduce.2.cloned.1.call-start = ((), (), s32[]{:S(2)}) async-start(), calls=%async_computation.5 | async-start | bytes 262144 | tf_op jit(solution)/shard_map/psum | solution.py:87
  146.6 59.0 %copy-start.2 = (bf16[32,256]{1,0:T(8,128)(2,1)}, bf16[32,256]{1,0:T(8,128)(2,1)S(1)}, u32[]{:S(2)}) copy-start(bf16[32,256]{1,0:T(8,128)(2,1)S(1)} %fusion.6) | copy-start | bytes 49156
Sparse Core Ops, SparseCore 0:
  225.8 64.9 all-reduce.1
